TPU v7x, 256 devices: a whole 4x4x8 slice. The times are simulated.
256 devices in a mesh: chan: 64 (over z, y_hi, x), win: 4 (over y_lo, core).
Axes of the slice: x: 4, y: 4 (y_hi: 2, y_lo: 2; y = y_hi * 2 + y_lo), z: 8, core: 2. Of those that a mesh axis runs over, the one named last changes fastest.
Arguments:
- traces: float32 [8, 2048, 2048], P('win', 'chan'), may hold values from -200 to 200
- quality: int32 [8, 2048], P('win', 'chan'), may hold values 0 or 1
Outputs:
- correlations: bfloat16 [2048, 2048, 128], P('chan', 'win')
Inputs may be any that keep to these rules, and one draw needn't show every extreme that they name: `quality`: 1 marks a usable window of a channel.
All inputs are finite; a program needn't handle non-finite values. No bound on the sum of `quality` on one device may be relied on, other than what follows from the above.
Results may differ from a plain program's by a relative error of at most 0.008.
Values may be sent and summed in bfloat16 or wider, within the bound.
No kernel may reach another device: no remote copies, remote signals or barrier semaphores. Data moves between devices by JAX's collectives and lax.ppermute only.
A program may use at most 128 MiB of HBM per device.

v0:
```python
import math
import jax
import jax.numpy as jnp
from jax import lax
from jax.sharding import PartitionSpec as P

SEGS = 8
NFFT = 256
F = 128
BAND = 8
LAGS = 128
epsilon = 1e-06
column_block = 512


def forward_table():
    sample_index = jnp.arange(NFFT, dtype=jnp.int32)[:, None]
    bin_index = jnp.arange(1, F + 1, dtype=jnp.int32)[None, :]
    angles = 2.0 * jnp.pi / NFFT * (sample_index * bin_index % NFFT).astype(jnp.float32)
    norm_scale = 1.0 / math.sqrt(NFFT)
    return jnp.concatenate([jnp.cos(angles), -jnp.sin(angles)], axis=1) * norm_scale


def lag_kernel(window_total):
    bin_index = jnp.arange(1, F + 1, dtype=jnp.int32)[:, None]
    lag_shift = jnp.arange(LAGS, dtype=jnp.int32)[None, :] - LAGS // 2
    angles = 2.0 * jnp.pi / NFFT * (bin_index * lag_shift % NFFT).astype(jnp.float32)
    norm_scale = 2.0 / math.sqrt(F * SEGS * window_total)
    return jnp.stack([jnp.cos(angles) * norm_scale, -jnp.sin(angles) * norm_scale]).astype(
        jnp.bfloat16
    )


def whiten(traces, quality):
    win_count, channels = (traces.shape[0], traces.shape[1])
    segments = traces.reshape(win_count, channels, SEGS, NFFT)
    spectrum = jnp.dot(segments, forward_table(), precision=lax.Precision.HIGHEST)
    real_part = spectrum[..., :F]
    imag_part = spectrum[..., F:]
    power_sum = (real_part * real_part + imag_part * imag_part).reshape(
        win_count, channels, SEGS, F // BAND, BAND
    )
    amplitude = jnp.sqrt(jnp.mean(power_sum, axis=(2, 4)) + epsilon)
    factor = quality.astype(jnp.float32)[:, :, None] / amplitude
    factor = jnp.repeat(factor, BAND, axis=2)[:, :, None, :]
    stacked_parts = jnp.stack([real_part * factor, imag_part * factor], axis=0)
    stacked_parts = jnp.transpose(stacked_parts, (2, 0, 1, 3, 4)).reshape(
        channels, 2 * win_count * SEGS, F
    )
    return stacked_parts.astype(jnp.bfloat16)


def rotate(spectra):
    middle = spectra.shape[1] // 2
    return jnp.concatenate([spectra[:, middle:], -spectra[:, :middle]], axis=1)


def block_lags(stacked, theirs, kernel):
    cross_part = jnp.einsum(
        "iwk,jwk->ijk", stacked, theirs, preferred_element_type=jnp.float32
    ).astype(jnp.bfloat16)
    cross_part = cross_part.reshape(2, stacked.shape[0] // 2, theirs.shape[0], cross_part.shape[-1])
    return jnp.einsum("pijk,pkt->jit", cross_part, kernel, preferred_element_type=jnp.float32)


def pair_lags(stacked, theirs, kernel):
    columns = theirs.shape[0]
    pieces = theirs.reshape(columns // column_block, column_block, theirs.shape[1], theirs.shape[2])
    lag_tiles = lax.map(lambda column_piece: block_lags(stacked, column_piece, kernel), pieces)
    return lag_tiles.reshape(columns, lag_tiles.shape[2], lag_tiles.shape[3])


def body(traces, quality):
    kernel = lag_kernel(lax.axis_size("win") * traces.shape[0])
    spectra = whiten(traces, quality)
    stacked = jnp.concatenate([spectra, rotate(spectra)], axis=0)
    partial_terms = pair_lags(stacked, lax.all_gather(spectra, "chan", axis=0, tiled=True), kernel)
    summed = lax.psum_scatter(
        partial_terms.astype(jnp.bfloat16), "win", scatter_dimension=0, tiled=True
    )
    return jnp.transpose(summed, (1, 0, 2))


def solution(mesh):
    in_specs = (P("win", "chan", None), P("win", "chan"))
    out_specs = P("chan", "win", None)
    return jax.shard_map(body, mesh=mesh, in_specs=in_specs, out_specs=out_specs, check_vma=False)
```

profile of v0, /device:TPU:1, one launch (start us, length us, event | category | flops | bytes accessed | tf_op | source)
XLA Modules:
  0.0 500.2 jit_solution(7143574307228338175)
XLA Ops:
  7.1 1.7 convolution_bitcast_fusion
  10.7 1.0 fusion.27
  11.7 1.0 maximum_maximum_fusion
  12.7 1.7 copy.27
  14.8 198.2 %all-gather.2.cloned.1.call-done = bf16[2048,32,128]{2,1,0:T(8,128)(2,1)} async-done(((bf16[32,32,128]{2,1,0:T(8,128)(2,1)}), bf16[2048,32,128]{2,1,0:T(8,128)(2,1)}) %all-gather.2.cloned.1.call-update) | async-done | bytes 16777232 | tf_op jit(solution)/shard_map/all_gather | solution.py:77
  212.9 119.6 %while.10 = (s32[]{:T(128)}, bf16[4,512,32,128]{3,1,2,0:T(8,128)(2,1)}, bf16[4,512,32,128]{3,2,1,0:T(8,128)(2,1)}, bf16[64,32,128]{0,1,2:T(8,128)(2,1)S(1)}, bf16[2,128,128]{2,1,0:T(8,128)(2,1)S(1)}, /*index=5*/s32[]{:T(128)}) while((s32[]{:T(128)}, bf16[4,512,32,128]{3,1,2,0:T(8,128)(2,1)}, bf16[4,512,32,128]{3,2,1,0:T(8,128)(2,1)}, ...), condition=%wide.region_3.4_spmd, body=%wide.region_2.3_spmd.sunk | while | flops 1346371584 | bytes 46727752 | solution.py:69
  212.9 4.9 constant_dynamic-slice_fusion.2
  217.9 8.6 %copy.44 = bf16[1,512,32,128]{1,2,3,0:T(8,128)(2,1)} copy(bf16[1,512,32,128]{3,2,1,0:T(8,128)(2,1)} %constant_dynamic-slice_fusion.2) | data formatting | bytes 8388608 | tf_op jit(solution)/shard_map/while/body/jit(dynamic_index_in_dim)/dynamic_slice | solution.py:69
  226.4 4.6 convolution_convert_fusion.2
  231.0 11.8 %bitcast_dynamic-update-slice_fusion.2 = bf16[4,512,32,128]{3,1,2,0:T(8,128)(2,1)} fusion(bf16[4,512,32,128]{3,1,2,0:T(8,128)(2,1)} %get-tuple-element.101, s32[]{:T(128)} %get-tuple-element.100, bf16[2,32,512,128]{2,1,0,3:T(8,128)(2,1)S(1)} %bitcast.52, bf16[2,128,128]{2,1,0:T(8,128)(2,1)S(1)} %get-tuple-element.110), kind=kOutput, calls=%fused_computation.clone.1 | convolution fusion | flops 1073741824 | bytes 16843264 | tf_op jit(solution)/shard_map/while/body/eval_jaxpr/pijk,pkt->jit/dot_general | solution.py:63
  242.8 4.9 constant_dynamic-slice_fusion.2
  247.8 8.6 %copy.44 = bf16[1,512,32,128]{1,2,3,0:T(8,128)(2,1)} copy(bf16[1,512,32,128]{3,2,1,0:T(8,128)(2,1)} %constant_dynamic-slice_fusion.2) | data formatting | bytes 8388608 | tf_op jit(solution)/shard_map/while/body/jit(dynamic_index_in_dim)/dynamic_slice | solution.py:69
  256.3 4.6 convolution_convert_fusion.2
  260.9 11.8 %bitcast_dynamic-update-slice_fusion.2 = bf16[4,512,32,128]{3,1,2,0:T(8,128)(2,1)} fusion(bf16[4,512,32,128]{3,1,2,0:T(8,128)(2,1)} %get-tuple-element.101, s32[]{:T(128)} %get-tuple-element.100, bf16[2,32,512,128]{2,1,0,3:T(8,128)(2,1)S(1)} %bitcast.52, bf16[2,128,128]{2,1,0:T(8,128)(2,1)S(1)} %get-tuple-element.110), kind=kOutput, calls=%fused_computation.clone.1 | convolution fusion | flops 1073741824 | bytes 16843264 | tf_op jit(solution)/shard_map/while/body/eval_jaxpr/pijk,pkt->jit/dot_general | solution.py:63
  272.8 4.9 constant_dynamic-slice_fusion.2
  277.7 8.6 %copy.44 = bf16[1,512,32,128]{1,2,3,0:T(8,128)(2,1)} copy(bf16[1,512,32,128]{3,2,1,0:T(8,128)(2,1)} %constant_dynamic-slice_fusion.2) | data formatting | bytes 8388608 | tf_op jit(solution)/shard_map/while/body/jit(dynamic_index_in_dim)/dynamic_slice | solution.py:69
  286.3 4.6 convolution_convert_fusion.2
  290.8 11.8 %bitcast_dynamic-update-slice_fusion.2 = bf16[4,512,32,128]{3,1,2,0:T(8,128)(2,1)} fusion(bf16[4,512,32,128]{3,1,2,0:T(8,128)(2,1)} %get-tuple-element.101, s32[]{:T(128)} %get-tuple-element.100, bf16[2,32,512,128]{2,1,0,3:T(8,128)(2,1)S(1)} %bitcast.52, bf16[2,128,128]{2,1,0:T(8,128)(2,1)S(1)} %get-tuple-element.110), kind=kOutput, calls=%fused_computation.clone.1 | convolution fusion | flops 1073741824 | bytes 16843264 | tf_op jit(solution)/shard_map/while/body/eval_jaxpr/pijk,pkt->jit/dot_general | solution.py:63
  302.7 4.9 constant_dynamic-slice_fusion.2
  307.6 8.6 %copy.44 = bf16[1,512,32,128]{1,2,3,0:T(8,128)(2,1)} copy(bf16[1,512,32,128]{3,2,1,0:T(8,128)(2,1)} %constant_dynamic-slice_fusion.2) | data formatting | bytes 8388608 | tf_op jit(solution)/shard_map/while/body/jit(dynamic_index_in_dim)/dynamic_slice | solution.py:69
  316.2 4.6 convolution_convert_fusion.2
  320.7 11.8 %bitcast_dynamic-update-slice_fusion.2 = bf16[4,512,32,128]{3,1,2,0:T(8,128)(2,1)} fusion(bf16[4,512,32,128]{3,1,2,0:T(8,128)(2,1)} %get-tuple-element.101, s32[]{:T(128)} %get-tuple-element.100, bf16[2,32,512,128]{2,1,0,3:T(8,128)(2,1)S(1)} %bitcast.52, bf16[2,128,128]{2,1,0:T(8,128)(2,1)S(1)} %get-tuple-element.110), kind=kOutput, calls=%fused_computation.clone.1 | convolution fusion | flops 1073741824 | bytes 16843264 | tf_op jit(solution)/shard_map/while/body/eval_jaxpr/pijk,pkt->jit/dot_general | solution.py:63
  332.6 13.9 %copy.28 = bf16[4,512,32,128]{3,1,0,2:T(8,128)(2,1)} copy(bf16[4,512,32,128]{3,1,2,0:T(8,128)(2,1)} %get-tuple-element.32) | data formatting | bytes 33554432 | tf_op jit(solution)/shard_map/convert_element_type | solution.py:79
  346.5 146.9 %reduce-scatter.2.cloned.1.call-done = bf16[512,32,128]{2,0,1:T(8,128)(2,1)} async-done(((bf16[2048,32,128]{2,0,1:T(8,128)(2,1)}), bf16[512,32,128]{2,0,1:T(8,128)(2,1)}) %reduce-scatter.2.cloned.1.call-update) | async-done | bytes 4194320 | tf_op jit(solution)/shard_map/reduce_scatter | solution.py:78
  (19 shorter events, 2.8 us)
Async XLA Ops:
  6.5 206.4 %all-gather.2.cloned.1.call-start = ((), (), s32[]{:S(2)}) async-start(), calls=%async_computation.1 | async-start | bytes 17039360 | tf_op jit(solution)/shard_map/all_gather | solution.py:77
  10.7 482.7 %reduce-scatter.2.cloned.1.call-start = ((), (), s32[]{:S(2)}) async-start(), calls=%async_computation.2 | async-start | bytes 20971520 | tf_op jit(solution)/shard_map/reduce_scatter | solution.py:78
Sparse Core Ops, SparseCore 0:
  11.0 201.9 all-gather.1
  346.6 146.7 reduce-scatter.1
where the time goes:
time: 501 us; the launch traced here: 500 us
  waiting for transfers between devices  345 us (69%)
  local copies, waits for them, and re-layouts  70.6 us (14%)
  matrix products  67.3 us (13%)
  between operations  13.5 us (3%)
    all_gather x1, waiting for transfers between devices, body(): lax.all_gather(spectra, 'chan', axis=0, tiled=True)  198 us
    reduce_scatter x1, waiting for transfers between devices, body(): lax.psum_scatter(partial_terms.astype(jnp.bfloat16), 'win', scatter_dimen...  147 us
    dynamic_slice x8, local copies, waits for them, and re-layouts, pair_lags(): lax.map(lambda column_piece: block_lags(stacked, column_piece, kernel), p...  54 us
    dot_general x4, matrix products, block_lags(): jnp.einsum('pijk,pkt->jit', cross_part, kernel, preferred_element_type=jn...  47.3 us
    dot_general x4, matrix products, block_lags(): jnp.einsum('iwk,jwk->ijk', stacked, theirs, preferred_element_type=jnp.fl...  18.3 us
    convert_element_type x1, local copies, waits for them, and re-layouts, body(): partial_terms.astype(jnp.bfloat16)  13.9 us
  transfers between devices with their start and end apart: 2, of which 2 were waited for; matrix products, arithmetic and copies ran while one was open for 1% of the time, Pallas kernels for 0%

commit v1 on v0

--- a/solution.py
+++ b/solution.py
@@ -71,10 +71,23 @@
 
 
 def body(traces, quality):
+
+    def treat_the_thing(my_tile):
+        odd = jnp.concatenate(
+            lax.all_to_all(
+                jnp.stack([my_tile for _ in range(lax.axis_size("chan"))]),
+                axis_name="chan",
+                split_axis=0,
+                concat_axis=0,
+            ),
+            axis=0,
+        )
+        return odd
+
     kernel = lag_kernel(lax.axis_size("win") * traces.shape[0])
     spectra = whiten(traces, quality)
     stacked = jnp.concatenate([spectra, rotate(spectra)], axis=0)
-    partial_terms = pair_lags(stacked, lax.all_gather(spectra, "chan", axis=0, tiled=True), kernel)
+    partial_terms = pair_lags(stacked, treat_the_thing(spectra), kernel)
     summed = lax.psum_scatter(
         partial_terms.astype(jnp.bfloat16), "win", scatter_dimension=0, tiled=True
     )

time: 501 us -> 709 us (1.42)
  waiting for transfers between devices: 345 us -> 533 us
  starting transfers between devices: 0.04 us -> 15.4 us
    all_to_all x0 -> x1, waiting for transfers between devices: none -> 376 us  [treat_the_thing(): lax.all_to_all(jnp.stack([my_tile for _ in range(lax.axis_size('chan'))])...]
    all_gather x1 -> x0, waiting for transfers between devices: 198 us -> none  [body(): lax.all_gather(spectra, 'chan', axis=0, tiled=True)]
    all_to_all x0 -> x1, starting transfers between devices: none -> 15.4 us  [treat_the_thing(): lax.all_to_all(jnp.stack([my_tile for _ in range(lax.axis_size('chan'))])...]
    reduce_scatter x1, waiting for transfers between devices: 147 us -> 157 us  [body(): lax.psum_scatter(partial_terms.astype(jnp.bfloat16), 'win', scatter_dimen...]
  transfers between devices with their start and end apart: 2 -> 2, of which waited for: 2 -> 2; matrix products, arithmetic and copies ran while one was open for 1% -> 0% of each run, Pallas kernels for 0% -> 0%
where the time goes in v1:
time: 709 us; the launch traced here: 707 us
  waiting for transfers between devices  533 us (75%)
  local copies, waits for them, and re-layouts  76.3 us (11%)
  matrix products  67.2 us (9%)
  starting transfers between devices  15.4 us (2%)
  between operations  13.5 us (2%)
    all_to_all x1, waiting for transfers between devices, treat_the_thing(): lax.all_to_all(jnp.stack([my_tile for _ in range(lax.axis_size('chan'))])...  376 us
    reduce_scatter x1, waiting for transfers between devices, body(): lax.psum_scatter(partial_terms.astype(jnp.bfloat16), 'win', scatter_dimen...  157 us
    dynamic_slice x8, local copies, waits for them, and re-layouts, pair_lags(): lax.map(lambda column_piece: block_lags(stacked, column_piece, kernel), p...  54 us
    dot_general x4, matrix products, block_lags(): jnp.einsum('pijk,pkt->jit', cross_part, kernel, preferred_element_type=jn...  47.3 us
    dot_general x4, matrix products, block_lags(): jnp.einsum('iwk,jwk->ijk', stacked, theirs, preferred_element_type=jnp.fl...  18.2 us
    all_to_all x1, starting transfers between devices, treat_the_thing(): lax.all_to_all(jnp.stack([my_tile for _ in range(lax.axis_size('chan'))])...  15.4 us
  transfers between devices with their start and end apart: 2, of which 2 were waited for; matrix products, arithmetic and copies ran while one was open for 0% of the time, Pallas kernels for 0%

profile of v1, /device:TPU:1, one launch (start us, length us, event | category | flops | bytes accessed | tf_op | source)
XLA Modules:
  0.0 707.3 jit_solution(17439674845995150249)
XLA Ops:
  7.1 1.7 convolution_bitcast_fusion
  9.9 6.3 stack.17
  16.2 15.4 %all-to-all-start = ((bf16[64,32,32,128]{3,2,1,0:T(8,128)(2,1)}), bf16[64,32,32,128]{3,2,1,0:T(8,128)(2,1)}, u32[]{:S(2)}, u32[]{:S(2)}) async-start(bf16[64,32,32,128]{3,2,1,0:T(8,128)(2,1)} %stack.17), calls=%async_computation | async-start | bytes 33554432 | tf_op jit(solution)/shard_map/all_to_all | solution.py:77
  31.7 1.7 copy.28
  33.8 375.9 %all-to-all-done = bf16[64,32,32,128]{3,2,1,0:T(8,128)(2,1)} async-done(((bf16[64,32,32,128]{3,2,1,0:T(8,128)(2,1)}), bf16[64,32,32,128]{3,2,1,0:T(8,128)(2,1)}, u32[]{:S(2)}, u32[]{:S(2)}) %all-to-all-start) | async-done | bytes 16777248 | tf_op jit(solution)/shard_map/all_to_all | solution.py:77
  409.7 119.6 %while.10 = (s32[]{:T(128)}, bf16[4,512,32,128]{3,1,2,0:T(8,128)(2,1)}, bf16[4,512,32,128]{3,2,1,0:T(8,128)(2,1)}, bf16[64,32,128]{0,1,2:T(8,128)(2,1)S(1)}, bf16[2,128,128]{2,1,0:T(8,128)(2,1)S(1)}, /*index=5*/s32[]{:T(128)}) while((s32[]{:T(128)}, bf16[4,512,32,128]{3,1,2,0:T(8,128)(2,1)}, bf16[4,512,32,128]{3,2,1,0:T(8,128)(2,1)}, ...), condition=%wide.region_3.4_spmd, body=%wide.region_2.3_spmd.sunk | while | flops 1346371584 | bytes 46727752 | solution.py:69
  409.7 4.9 constant_dynamic-slice_fusion.2
  414.6 8.6 %copy.45 = bf16[1,512,32,128]{1,2,3,0:T(8,128)(2,1)} copy(bf16[1,512,32,128]{3,2,1,0:T(8,128)(2,1)} %constant_dynamic-slice_fusion.2) | data formatting | bytes 8388608 | tf_op jit(solution)/shard_map/while/body/jit(dynamic_index_in_dim)/dynamic_slice | solution.py:69
  423.2 4.6 convolution_convert_fusion.2
  427.8 11.8 %bitcast_dynamic-update-slice_fusion.2 = bf16[4,512,32,128]{3,1,2,0:T(8,128)(2,1)} fusion(bf16[4,512,32,128]{3,1,2,0:T(8,128)(2,1)} %get-tuple-element.101, s32[]{:T(128)} %get-tuple-element.100, bf16[2,32,512,128]{2,1,0,3:T(8,128)(2,1)S(1)} %bitcast.52, bf16[2,128,128]{2,1,0:T(8,128)(2,1)S(1)} %get-tuple-element.110), kind=kOutput, calls=%fused_computation.clone.1 | convolution fusion | flops 1073741824 | bytes 16843264 | tf_op jit(solution)/shard_map/while/body/eval_jaxpr/pijk,pkt->jit/dot_general | solution.py:63
  439.6 4.9 constant_dynamic-slice_fusion.2
  444.5 8.6 %copy.45 = bf16[1,512,32,128]{1,2,3,0:T(8,128)(2,1)} copy(bf16[1,512,32,128]{3,2,1,0:T(8,128)(2,1)} %constant_dynamic-slice_fusion.2) | data formatting | bytes 8388608 | tf_op jit(solution)/shard_map/while/body/jit(dynamic_index_in_dim)/dynamic_slice | solution.py:69
  453.1 4.6 convolution_convert_fusion.2
  457.7 11.9 %bitcast_dynamic-update-slice_fusion.2 = bf16[4,512,32,128]{3,1,2,0:T(8,128)(2,1)} fusion(bf16[4,512,32,128]{3,1,2,0:T(8,128)(2,1)} %get-tuple-element.101, s32[]{:T(128)} %get-tuple-element.100, bf16[2,32,512,128]{2,1,0,3:T(8,128)(2,1)S(1)} %bitcast.52, bf16[2,128,128]{2,1,0:T(8,128)(2,1)S(1)} %get-tuple-element.110), kind=kOutput, calls=%fused_computation.clone.1 | convolution fusion | flops 1073741824 | bytes 16843264 | tf_op jit(solution)/shard_map/while/body/eval_jaxpr/pijk,pkt->jit/dot_general | solution.py:63
  469.5 4.9 constant_dynamic-slice_fusion.2
  474.4 8.6 %copy.45 = bf16[1,512,32,128]{1,2,3,0:T(8,128)(2,1)} copy(bf16[1,512,32,128]{3,2,1,0:T(8,128)(2,1)} %constant_dynamic-slice_fusion.2) | data formatting | bytes 8388608 | tf_op jit(solution)/shard_map/while/body/jit(dynamic_index_in_dim)/dynamic_slice | solution.py:69
  483.0 4.6 convolution_convert_fusion.2
  487.6 11.8 %bitcast_dynamic-update-slice_fusion.2 = bf16[4,512,32,128]{3,1,2,0:T(8,128)(2,1)} fusion(bf16[4,512,32,128]{3,1,2,0:T(8,128)(2,1)} %get-tuple-element.101, s32[]{:T(128)} %get-tuple-element.100, bf16[2,32,512,128]{2,1,0,3:T(8,128)(2,1)S(1)} %bitcast.52, bf16[2,128,128]{2,1,0:T(8,128)(2,1)S(1)} %get-tuple-element.110), kind=kOutput, calls=%fused_computation.clone.1 | convolution fusion | flops 1073741824 | bytes 16843264 | tf_op jit(solution)/shard_map/while/body/eval_jaxpr/pijk,pkt->jit/dot_general | solution.py:63
  499.4 4.9 constant_dynamic-slice_fusion.2
  504.3 8.6 %copy.45 = bf16[1,512,32,128]{1,2,3,0:T(8,128)(2,1)} copy(bf16[1,512,32,128]{3,2,1,0:T(8,128)(2,1)} %constant_dynamic-slice_fusion.2) | data formatting | bytes 8388608 | tf_op jit(solution)/shard_map/while/body/jit(dynamic_index_in_dim)/dynamic_slice | solution.py:69
  512.9 4.6 convolution_convert_fusion.2
  517.5 11.8 %bitcast_dynamic-update-slice_fusion.2 = bf16[4,512,32,128]{3,1,2,0:T(8,128)(2,1)} fusion(bf16[4,512,32,128]{3,1,2,0:T(8,128)(2,1)} %get-tuple-element.101, s32[]{:T(128)} %get-tuple-element.100, bf16[2,32,512,128]{2,1,0,3:T(8,128)(2,1)S(1)} %bitcast.52, bf16[2,128,128]{2,1,0:T(8,128)(2,1)S(1)} %get-tuple-element.110), kind=kOutput, calls=%fused_computation.clone.1 | convolution fusion | flops 1073741824 | bytes 16843264 | tf_op jit(solution)/shard_map/while/body/eval_jaxpr/pijk,pkt->jit/dot_general | solution.py:63
  529.3 13.9 %copy.29 = bf16[4,512,32,128]{3,1,0,2:T(8,128)(2,1)} copy(bf16[4,512,32,128]{3,1,2,0:T(8,128)(2,1)} %get-tuple-element.32) | data formatting | bytes 33554432 | tf_op jit(solution)/shard_map/convert_element_type | solution.py:92
  543.3 157.1 %reduce-scatter.2.cloned.1.call-done = bf16[512,32,128]{2,0,1:T(8,128)(2,1)} async-done(((bf16[2048,32,128]{2,0,1:T(8,128)(2,1)}), bf16[512,32,128]{2,0,1:T(8,128)(2,1)}) %reduce-scatter.2.cloned.1.call-update) | async-done | bytes 4194320 | tf_op jit(solution)/shard_map/reduce_scatter | solution.py:91
  (19 shorter events, 2.2 us)
Async XLA Ops:
  16.2 393.5 %all-to-all-start = ((bf16[64,32,32,128]{3,2,1,0:T(8,128)(2,1)}), bf16[64,32,32,128]{3,2,1,0:T(8,128)(2,1)}, u32[]{:S(2)}, u32[]{:S(2)}) async-start(bf16[64,32,32,128]{3,2,1,0:T(8,128)(2,1)} %stack.17), calls=%async_computation | async-start | bytes 33554432 | tf_op jit(solution)/shard_map/all_to_all | solution.py:77
  31.6 668.8 %reduce-scatter.2.cloned.1.call-start = ((), (), s32[]{:S(2)}) async-start(), calls=%async_computation.2 | async-start | bytes 20971520 | tf_op jit(solution)/shard_map/reduce_scatter | solution.py:91
Sparse Core Ops, SparseCore 0:
  543.4 156.9 reduce-scatter.1
